TPU v7x, 128 devices: a whole 4x4x4 slice. The times are simulated.
128 devices in a mesh: req: 32 (over x, z, core), tensor: 4 (over y).
Axes of the slice: x: 4, y: 4, z: 4, core: 2. Of those that a mesh axis runs over, the one named last changes fastest.
Arguments:
- hidden_in: bfloat16 [32768, 2048], P('req', 'tensor'), may hold values from -6 to 6
- segment: int32 [32768], P('req'), may hold values from 0 to 15, never falling along the last dimension, each value on 1 to 4096 neighbouring positions
- w_query: bfloat16 [2048, 1024], P(None, 'tensor'), may hold values from -0.125 to 0.125
- w_key: bfloat16 [2048, 1024], P(None, 'tensor'), may hold values from -0.125 to 0.125
- w_value: bfloat16 [2048, 2048], P(None, 'tensor'), may hold values from -0.125 to 0.125
- w_outgate: bfloat16 [2048, 2048], P(None, 'tensor'), may hold values from -0.125 to 0.125
- w_gate_down: bfloat16 [2048, 16], replicated, may hold values from -0.125 to 0.125
- w_gate_up: bfloat16 [16, 1024], P(None, 'tensor'), may hold values from -1.5 to 1.5
- gate_bias: float32 [1024], P('tensor'), may hold values from -2 to 8
- norm_gain: float32 [512], replicated, may hold values from 0.5 to 1.5
- w_out: bfloat16 [2048, 2048], P('tensor'), may hold values from -0.125 to 0.125
Outputs:
- mixed: bfloat16 [32768, 2048], P('req', 'tensor')
Inputs may be any that keep to these rules, and one draw needn't show every extreme that they name: segment never falls along the tokens; each prompt covers 1 to 4096 consecutive tokens and one covers exactly 4096.
All inputs are finite; a program needn't handle non-finite values.
Results may differ from a plain program's by a relative error of at most 0.014.
Values may be sent and summed in bfloat16 or wider, within the bound.
No kernel may reach another device: no remote copies, remote signals or barrier semaphores. Data moves between devices by JAX's collectives and lax.ppermute only.
A program may use at most 128 MiB of HBM per device.

v0:
```python
import jax
import jax.numpy as jnp
from jax import lax
from jax.sharding import PartitionSpec as P

GROUP = 64


def carried_in(shard, axis, combine, identity):
    devices, index = (lax.axis_size(axis), lax.axis_index(axis))
    everything = jax.tree.map(
        lambda part, kind: lax.all_gather(part.astype(kind), axis),
        shard,
        jax.tree.map(lambda a: jnp.bfloat16 if a.dtype == jnp.float32 else a.dtype, shard),
    )
    start = jax.tree.map(
        lambda part, zero: jnp.broadcast_to(jnp.asarray(zero, part.dtype), part.shape),
        shard,
        identity,
    )

    def lap(k, before):
        reached = k < index
        new = combine(
            before, jax.tree.map(lambda part, own: part[k].astype(own.dtype), everything, shard)
        )
        return jax.tree.map(lambda a, b: jnp.where(reached, a, b), new, before)

    return lax.fori_loop(0, devices, lap, start)


def combine(earlier, later):
    first_a, last_a, decay_a, state_a = earlier
    first_b, last_b, decay_b, state_b = later
    linked = ((first_b == last_a) | (last_a == 0.0) | (first_b == 0.0)).astype(jnp.float32)
    decay_new = decay_b * decay_a * linked
    state_new = state_b + (linked * decay_b)[:, None] * state_a
    first_new = jnp.where(first_a > 0.0, first_a, first_b)
    last_new = jnp.where(last_b > 0.0, last_b, last_a)
    return (first_new, last_new, decay_new, state_new)


def body(
    hidden_in,
    segment,
    w_query,
    w_key,
    w_value,
    w_outgate,
    w_gate_down,
    w_gate_up,
    gate_bias,
    norm_gain,
    w_out,
):
    tok_rows = hidden_in.shape[0]
    key_width = w_query.shape[1]
    value_width = w_value.shape[1]
    weights = (w_query, w_key, w_value, w_outgate, w_gate_down)
    piece = lax.all_gather(hidden_in, "tensor", axis=1, tiled=True)
    query_sum, key_sum, value_sum, outgate, low = tuple(
        (jnp.dot(piece, weight, preferred_element_type=jnp.float32) for weight in weights)
    )
    query = query_sum.astype(jnp.bfloat16)
    key = key_sum.astype(jnp.bfloat16)
    value = value_sum.astype(jnp.bfloat16)
    pre_gate = (
        jnp.dot(low, w_gate_up.astype(jnp.float32), precision=lax.Precision.HIGHEST) + gate_bias
    )
    logdecay = jax.nn.log_sigmoid(pre_gate) / 16.0
    blocks = tok_rows // GROUP
    starts = jnp.concatenate(
        [jnp.zeros((1,), jnp.int32), (segment[1:] != segment[:-1]).astype(jnp.int32)]
    )
    live_device = (jnp.cumsum(starts) == 0).astype(jnp.float32)
    seg_blocks = segment.reshape(blocks, GROUP)
    live_blocks = (jnp.cumsum(starts.reshape(blocks, GROUP), axis=1) == 0).astype(jnp.float32)
    cumul = jnp.cumsum(logdecay.reshape(blocks, GROUP, key_width), axis=1)
    block_totals = cumul[:, -1, :]
    before = jnp.cumsum(block_totals, axis=0) - block_totals
    device_cumul = (cumul + before[:, None, :]).reshape(tok_rows, key_width)
    positions = jnp.arange(GROUP)
    causal = positions[None, :] <= positions[:, None]
    middle_row = GROUP // 2

    def block_step(state, inputs):
        q_block, k_block, v_block, c_block, s_block, l_block = inputs
        q_float = q_block.astype(jnp.float32)
        k_float = k_block.astype(jnp.float32)
        v_float = v_block.astype(jnp.float32)
        inter = (
            jnp.dot(q_float * jnp.exp(c_block), state, precision=lax.Precision.HIGHEST)
            * l_block[:, None]
        )
        allowed = causal & (s_block[:, None] == s_block[None, :])
        centre = c_block[middle_row]
        q_scaled = q_float * jnp.exp(c_block - centre[None, :])
        k_scaled = k_float * jnp.exp(centre[None, :] - c_block)
        raw_scores = jnp.dot(q_scaled, k_scaled.T, precision=lax.Precision.HIGHEST)
        scores = jnp.where(allowed, raw_scores, 0.0)
        intra = jnp.dot(scores, v_float, precision=lax.Precision.HIGHEST)
        last_cumul = c_block[-1]
        same_last = (s_block == s_block[-1]).astype(jnp.float32)
        k_decayed = k_float * jnp.exp(last_cumul[None, :] - c_block) * same_last[:, None]
        state = l_block[-1] * jnp.exp(last_cumul)[:, None] * state + jnp.dot(
            k_decayed.T, v_float, precision=lax.Precision.HIGHEST
        )
        return (state, inter + intra)

    zero_state = jnp.zeros((key_width, value_width), jnp.float32)
    final_state, local_out = lax.scan(
        block_step,
        zero_state,
        (
            query.reshape(blocks, GROUP, key_width),
            key.reshape(blocks, GROUP, key_width),
            value.reshape(blocks, GROUP, value_width),
            cumul,
            seg_blocks,
            live_blocks,
        ),
    )
    local_out = local_out.reshape(tok_rows, value_width)
    first_id = (segment[0] + 1).astype(jnp.float32)
    last_id = (segment[-1] + 1).astype(jnp.float32)
    decay_device = jnp.exp(device_cumul[-1]) * live_device[-1]
    mine = (first_id, last_id, decay_device, final_state)
    identity = (
        jnp.zeros((), jnp.float32),
        jnp.zeros((), jnp.float32),
        jnp.ones((key_width,), jnp.float32),
        jnp.zeros((key_width, value_width), jnp.float32),
    )
    incoming = carried_in(mine, "req", combine, identity)
    first_in, last_in, decay_in, state_in = incoming
    linked = ((first_id == last_in) | (last_in == 0.0)).astype(jnp.float32)
    carried = jnp.dot(
        query.astype(jnp.float32) * jnp.exp(device_cumul), state_in, precision=lax.Precision.HIGHEST
    )
    attn = (local_out + carried * (live_device * linked)[:, None]) * key_width ** (-0.5)
    normed = attn * lax.rsqrt(jnp.mean(attn * attn, axis=-1, keepdims=True) + 1e-05) * norm_gain
    gated = (normed * jax.nn.silu(outgate)).astype(jnp.bfloat16)
    head_term = jnp.dot(gated, w_out, preferred_element_type=jnp.float32)
    return lax.psum_scatter(
        head_term.astype(jnp.bfloat16), "tensor", scatter_dimension=1, tiled=True
    )


def solution(mesh):
    in_specs = (
        P("req", "tensor"),
        P("req"),
        P(None, "tensor"),
        P(None, "tensor"),
        P(None, "tensor"),
        P(None, "tensor"),
        P(),
        P(None, "tensor"),
        P("tensor"),
        P(),
        P("tensor", None),
    )
    out_specs = P("req", "tensor")
    return jax.shard_map(body, mesh=mesh, in_specs=in_specs, out_specs=out_specs, check_vma=False)
```

profile of v0, /device:TPU:1, one launch (start us, length us, event | category | flops | bytes accessed | tf_op | source)
XLA Modules:
  0.0 539.6 jit_solution(2485547177089798620)
XLA Ops:
  9.3 51.0 %all-gather.5.cloned.1.call-done = bf16[1024,2048]{1,0:T(8,128)(2,1)} async-done(((bf16[1024,512]{1,0:T(8,128)(2,1)}), bf16[1024,2048]{1,0:T(8,128)(2,1)}) %all-gather.5.cloned.1.call-update) | async-done | bytes 4194320 | tf_op jit(solution)/shard_map/all_gather | solution.py:60
  60.3 3.4 fusion.69
  63.7 1.2 fusion.48
  64.9 1.6 fusion.49
  66.5 1.3 convolution_convert_fusion.2
  68.0 3.4 convolution_convert_fusion.1
  71.4 2.0 convolution_convert_fusion.3
  73.5 133.2 %while.29 = (s32[]{:T(128)}, f32[256,512]{1,0:T(8,128)S(1)}, f32[16,64,512]{2,1,0:T(8,128)}, f32[16,64]{1,0:T(8,128)S(1)}, f32[16,64,256]{2,0,1:T(8,128)}, /*ind...) while((s32[]{:T(128)}, f32[256,512]{1,0:T(8,128)S(1)}, ...), condition=%wide.region_3.4_spmd.clone, body=%wide.region_2.3_spmd.clone.sunk | while | flops 239878528 | bytes 2676648 | solution.py:111
  73.5 1.1 constant_dynamic-slice_fusion.6
  76.7 1.1 fusion.114
  80.4 1.4 convolution_add_fusion.3
  81.8 1.1 constant_dynamic-slice_fusion.6
  85.0 1.1 fusion.114
  88.7 1.4 convolution_add_fusion.3
  90.1 1.1 constant_dynamic-slice_fusion.6
  93.3 1.1 fusion.114
  97.0 1.4 convolution_add_fusion.3
  98.4 1.1 constant_dynamic-slice_fusion.6
  101.6 1.1 fusion.114
  105.3 1.4 convolution_add_fusion.3
  106.8 1.1 constant_dynamic-slice_fusion.6
  110.0 1.1 fusion.114
  113.7 1.4 convolution_add_fusion.3
  115.1 1.1 constant_dynamic-slice_fusion.6
  118.3 1.1 fusion.114
  122.0 1.4 convolution_add_fusion.3
  123.4 1.1 constant_dynamic-slice_fusion.6
  126.6 1.1 fusion.114
  130.3 1.4 convolution_add_fusion.3
  131.7 1.1 constant_dynamic-slice_fusion.6
  134.9 1.1 fusion.114
  138.6 1.4 convolution_add_fusion.3
  140.1 1.1 constant_dynamic-slice_fusion.6
  143.3 1.1 fusion.114
  147.0 1.4 convolution_add_fusion.3
  148.4 1.1 constant_dynamic-slice_fusion.6
  151.6 1.1 fusion.114
  155.3 1.4 convolution_add_fusion.3
  159.9 1.1 fusion.114
  163.6 1.4 convolution_add_fusion.3
  165.1 1.1 constant_dynamic-slice_fusion.6
  168.2 1.1 fusion.114
  171.9 1.4 convolution_add_fusion.3
  173.4 1.1 constant_dynamic-slice_fusion.6
  176.6 1.1 fusion.114
  180.2 1.4 convolution_add_fusion.3
  184.9 1.1 fusion.114
  188.6 1.4 convolution_add_fusion.3
  190.0 1.1 constant_dynamic-slice_fusion.6
  193.2 1.1 fusion.114
  196.9 1.4 convolution_add_fusion.3
  198.3 1.1 constant_dynamic-slice_fusion.6
  201.5 1.1 fusion.114
  205.2 1.4 convolution_add_fusion.3
  207.5 1.4 fusion.66
  211.0 1.4 dynamic-update-slice
  212.4 63.8 %all-reduce.2 = (bf16[32]{0:T(256)(128)(2,1)S(1)}, bf16[32]{0:T(256)(128)(2,1)S(1)}) all-reduce(bf16[32]{0:T(256)(128)(2,1)S(1)} %dynamic-update-slice, bf16[32]{0:T(256)(128)(2,1)S(1)} %dynamic-update-slice.1), channel_id=1, replica_groups=mesh['req'=32,'tensor'=4] {'req'}, use_global_device_ids=true, to_apply=%add | all-reduce | flops 64 | bytes 256
  279.6 1.3 broadcast_add_fusion
  282.5 25.4 %all-gather.1 = bf16[32,1,256]{2,1,0:T(2,128)(2,1)S(1)} all-gather(bf16[1,1,256]{2,1,0:T(2,128)(2,1)S(1)} %fusion.62), channel_id=1, replica_groups=mesh['req'=32,'tensor'=4] {'req'}, dimensions={0}, use_global_device_ids=true | all-gather | bytes 16896 | tf_op jit(solution)/shard_map/all_gather | solution.py:12
  307.9 2.9 copy.41
  310.8 160.3 %while.30 = (s32[]{:T(128)}, f32[]{:T(128)}, f32[256,512]{1,0:T(8,128)S(1)}, s32[]{:T(128)}, bf16[32]{0:T(256)(128)(2,1)S(1)}, /*index=5*/bf16[32,256,512]{2,1,0...) while((s32[]{:T(128)}, f32[]{:T(128)}, ...), condition=%wide.region_8.9_spmd.clone, body=%wide.region_7.8_spmd.clone.sunk | while | flops 655885 | bytes 1313502 | solution.py:29
  471.2 5.6 %multiply_reduce_fusion = (f32[1024]{0:T(1024)S(1)}, f32[1024,512]{0,1:T(8,128)}) fusion(f32[1024,512]{0,1:T(8,128)} %copy.41, f32[1024]{0:T(1024)S(1)} %select_bitcast_fusion, f32[256,512]{1,0:T(8,128)S(1)} %get-tuple-element.200, f32[1024,256]{1,0:T(8,128)} %bitcast.116, bf16[1024,256]{1,0:T(8,128)(2,1)S(1)} %bitcast.119), kind=kOutput, calls=%fused_computation.59 | convolution fusion | flops 1613757440 | bytes 6299648 | tf_op jit(solution)/shard_map/dot_general | solution.py:137
  476.8 10.3 %convolution_convert_fusion = bf16[1024,2048]{1,0:T(8,128)(2,1)} fusion(bf16[512,2048]{1,0:T(8,128)(2,1)S(1)} %copy-done, f32[1024,512]{0,1:T(8,128)} %get-tuple-element.340, f32[512]{0:T(512)S(1)} %copy-done.7, f32[1024]{0:T(1024)S(1)} %rsqrt_multiply_fusion, bf16[1024,2048]{1,0:T(8,128)(2,1)} %all-gather.5.cloned.1.call-done, bf16[2048,512]{1,0:T(8,128)(2,1)} %param.20), kind=kOutput, calls=%fused_computation.56 | convolution fusion | flops 4301258752 | bytes 14686208 | tf_op jit(solution)/shard_map/dot_general | solution.py:143
  487.2 46.0 %reduce-scatter.2.cloned.1.call-done = bf16[1024,512]{1,0:T(8,128)(2,1)} async-done(((bf16[1024,2048]{1,0:T(8,128)(2,1)}), bf16[1024,512]{1,0:T(8,128)(2,1)}) %reduce-scatter.2.cloned.1.call-update) | async-done | bytes 1048592 | tf_op jit(solution)/shard_map/reduce_scatter | solution.py:144
  (393 shorter events, 162.6 us)
Async XLA Ops:
  6.5 470.3 %copy-start = (bf16[512,2048]{1,0:T(8,128)(2,1)S(1)}, bf16[512,2048]{1,0:T(8,128)(2,1)}, u32[]{:S(2)}) copy-start(bf16[512,2048]{1,0:T(8,128)(2,1)} %param.25) | copy-start | bytes 6291460
  6.5 53.7 %all-gather.5.cloned.1.call-start = ((), (), s32[]{:S(2)}) async-start(), calls=%async_computation.1 | async-start | bytes 5242880 | tf_op jit(solution)/shard_map/all_gather | solution.py:60
  7.3 303.5 %all-gather.7.cloned.1.call-start = ((), (), s32[]{:S(2)}) async-start(), calls=%async_computation.3 | async-start | bytes 8650752 | tf_op jit(solution)/shard_map/all_gather | solution.py:12
  9.3 54.4 %copy-start.6 = (bf16[16,256]{1,0:T(8,128)(2,1)S(1)}, bf16[16,256]{1,0:T(8,128)(2,1)}, u32[]{:S(2)}) copy-start(bf16[16,256]{1,0:T(8,128)(2,1)} %param.22) | copy-start | bytes 24580
  9.3 54.4 %copy-start.8 = (f32[256]{0:T(256)S(1)}, f32[256]{0:T(256)}, u32[]{:S(2)}) copy-start(f32[256]{0:T(256)} %param.23) | copy-start | bytes 3076
  63.7 2.8 copy-start.1
  63.7 2.8 copy-start.4
  66.4 1.6 copy-start.3
  68.0 3.4 copy-start.5
  73.5 136.1 %copy-start.9 = (u32[128]{0:T(128)S(1)}, u32[128]{0:T(128)}, u32[]{:S(2)}) copy-start(u32[128]{0:T(128)} %constant.99) | copy-start | bytes 1540
  207.4 325.7 %reduce-scatter.2.cloned.1.call-start = ((), (), s32[]{:S(2)}) async-start(), calls=%async_computation.2 | async-start | bytes 5242880 | tf_op jit(solution)/shard_map/reduce_scatter | solution.py:144
  281.5 1.0 copy-start.2
  471.2 5.6 %copy-start.7 = (f32[512]{0:T(512)S(1)}, f32[512]{0:T(512)}, u32[]{:S(2)}) copy-start(f32[512]{0:T(512)} %param.24) | copy-start | bytes 6148
Sparse Core Ops, SparseCore 0:
  9.0 51.2 all-gather.4
  207.5 53.9 all-gather.6
  487.3 45.7 reduce-scatter.1
where the time goes:
time: 546 us; the launch traced here: 540 us
  matrix products  99.8 us (18%)
  waiting for transfers between devices  97.7 us (18%)
  local copies, waits for them, and re-layouts  90.8 us (17%)
  blocking collectives  89.2 us (16%)
  loops' own time  84.8 us (16%)
  other arithmetic  62.7 us (11%)
  between operations  14.6 us (3%)
    another operation x1, loops' own time, carried_in(): return lax.fori_loop(0, devices, lap, start)  83.2 us
    unnamed x1, blocking collectives  63.8 us
    all_gather x1, waiting for transfers between devices, body(): piece = lax.all_gather(hidden_in, 'tensor', axis=1, tiled=True)  51 us
    reduce_scatter x1, waiting for transfers between devices, body(): lax.psum_scatter(head_term.astype(jnp.bfloat16), 'tensor', scatter_dimens...  46 us
    dynamic_slice x64, local copies, waits for them, and re-layouts, lap(): part[k].astype(own.dtype)  41.7 us
    select_n x32, other arithmetic, lap(): return jax.tree.map(lambda a, b: jnp.where(reached, a, b), new, before)  34.9 us
    all_gather x1, blocking collectives, carried_in(): lax.all_gather(part.astype(kind), axis)  25.4 us
    dot_general x16, matrix products, block_step(): jnp.dot(k_decayed.T, v_float, precision=lax.Precision.HIGHEST)  22.6 us
  transfers between devices with their start and end apart: 3, of which 2 were waited for; matrix products, arithmetic and copies ran while one was open for 3% of the time, Pallas kernels for 0%

commit v1 on v0

--- a/solution.py
+++ b/solution.py
@@ -57,7 +57,9 @@
     key_width = w_query.shape[1]
     value_width = w_value.shape[1]
     weights = (w_query, w_key, w_value, w_outgate, w_gate_down)
-    piece = lax.all_gather(hidden_in, "tensor", axis=1, tiled=True)
+    piece = jnp.concatenate(
+        lax.all_to_all(jnp.stack([hidden_in] * lax.axis_size("tensor")), "tensor", 0, 0), axis=1
+    )
     query_sum, key_sum, value_sum, outgate, low = tuple(
         (jnp.dot(piece, weight, preferred_element_type=jnp.float32) for weight in weights)
     )

time: 546 us -> 556 us (1.018)
  matrix products: 99.8 us -> 106 us
    all_gather x1 -> x0, waiting for transfers between devices: 51 us -> none  [body(): piece = lax.all_gather(hidden_in, 'tensor', axis=1, tiled=True)]
    all_to_all x0 -> x1, waiting for transfers between devices: none -> 48.3 us  [body(): lax.all_to_all(jnp.stack([hidden_in] * lax.axis_size('tensor')), 'tensor'...]
    dot_general x4, matrix products: 10 us -> 16.5 us  [body(): jnp.dot(piece, weight, preferred_element_type=jnp.float32)]
  transfers between devices with their start and end apart: 3 -> 3, of which waited for: 2 -> 2; matrix products, arithmetic and copies ran while one was open for 3% -> 2% of each run, Pallas kernels for 0% -> 0%
where the time goes in v1:
time: 556 us; the launch traced here: 550 us
  matrix products  106 us (19%)
  local copies, waits for them, and re-layouts  93.9 us (17%)
  waiting for transfers between devices  93.5 us (17%)
  blocking collectives  90.5 us (16%)
  loops' own time  84.8 us (15%)
  other arithmetic  61.2 us (11%)
  between operations  14.9 us (3%)
    another operation x1, loops' own time, carried_in(): return lax.fori_loop(0, devices, lap, start)  83.2 us
    unnamed x1, blocking collectives  65.9 us
    all_to_all x1, waiting for transfers between devices, body(): lax.all_to_all(jnp.stack([hidden_in] * lax.axis_size('tensor')), 'tensor'...  48.3 us
    reduce_scatter x1, waiting for transfers between devices, body(): lax.psum_scatter(head_term.astype(jnp.bfloat16), 'tensor', scatter_dimens...  45.1 us
    dynamic_slice x64, local copies, waits for them, and re-layouts, lap(): part[k].astype(own.dtype)  41.7 us
    select_n x32, other arithmetic, lap(): return jax.tree.map(lambda a, b: jnp.where(reached, a, b), new, before)  34.9 us
    all_gather x1, blocking collectives, carried_in(): lax.all_gather(part.astype(kind), axis)  24.6 us
    dot_general x16, matrix products, block_step(): jnp.dot(k_decayed.T, v_float, precision=lax.Precision.HIGHEST)  22.6 us
  transfers between devices with their start and end apart: 3, of which 2 were waited for; matrix products, arithmetic and copies ran while one was open for 2% of the time, Pallas kernels for 0%

profile of v1, /device:TPU:1, one launch (start us, length us, event | category | flops | bytes accessed | tf_op | source)
XLA Modules:
  0.0 550.1 jit_solution(12630388079054616347)
XLA Ops:
  6.5 1.6 copy.38
  8.2 2.5 stack.2
  10.7 5.1 all-to-all-start
  16.3 48.3 %all-to-all-done = bf16[4,1024,512]{1,2,0:T(8,128)(2,1)} async-done(((bf16[4,1024,512]{1,2,0:T(8,128)(2,1)}), bf16[4,1024,512]{1,2,0:T(8,128)(2,1)}, u32[]{:S(2)}, u32[]{:S(2)}) %all-to-all-start) | async-done | bytes 4194336 | tf_op jit(solution)/shard_map/all_to_all | solution.py:61
  64.7 2.9 fusion.69
  67.6 1.2 fusion.48
  68.7 1.6 fusion.49
  70.3 3.7 convolution_convert_fusion.2
  74.0 5.7 %convolution_convert_fusion.1 = bf16[1024,512]{1,0:T(8,128)(2,1)} fusion(bf16[1024,2048]{0,1:T(8,128)(2,1)} %bitcast.1, bf16[2048,512]{1,0:T(8,128)(2,1)S(1)} %copy-done.4), kind=kOutput, calls=%fused_computation.61 | convolution fusion | flops 2148007936 | bytes 7340032 | tf_op jit(solution)/shard_map/dot_general | solution.py:64
  79.7 4.3 convolution_convert_fusion.3
  84.0 133.2 %while.29 = (s32[]{:T(128)}, f32[256,512]{1,0:T(8,128)S(1)}, f32[16,64,512]{2,1,0:T(8,128)}, f32[16,64]{1,0:T(8,128)S(1)}, f32[16,64,256]{2,0,1:T(8,128)}, /*ind...) while((s32[]{:T(128)}, f32[256,512]{1,0:T(8,128)S(1)}, ...), condition=%wide.region_3.4_spmd.clone, body=%wide.region_2.3_spmd.clone.sunk | while | flops 239878528 | bytes 2676648 | solution.py:113
  84.0 1.1 constant_dynamic-slice_fusion.6
  87.2 1.1 fusion.114
  90.9 1.4 convolution_add_fusion.3
  95.5 1.1 fusion.114
  99.2 1.4 convolution_add_fusion.3
  100.6 1.1 constant_dynamic-slice_fusion.6
  103.8 1.1 fusion.114
  107.5 1.4 convolution_add_fusion.3
  109.0 1.1 constant_dynamic-slice_fusion.6
  112.2 1.1 fusion.114
  115.9 1.4 convolution_add_fusion.3
  117.3 1.1 constant_dynamic-slice_fusion.6
  120.5 1.1 fusion.114
  124.2 1.4 convolution_add_fusion.3
  125.6 1.1 constant_dynamic-slice_fusion.6
  128.8 1.1 fusion.114
  132.5 1.4 convolution_add_fusion.3
  137.1 1.1 fusion.114
  140.8 1.4 convolution_add_fusion.3
  145.5 1.1 fusion.114
  149.2 1.4 convolution_add_fusion.3
  150.6 1.1 constant_dynamic-slice_fusion.6
  153.8 1.1 fusion.114
  157.5 1.4 convolution_add_fusion.3
  162.1 1.1 fusion.114
  165.8 1.4 convolution_add_fusion.3
  167.2 1.1 constant_dynamic-slice_fusion.6
  170.4 1.1 fusion.114
  174.1 1.4 convolution_add_fusion.3
  175.6 1.1 constant_dynamic-slice_fusion.6
  178.8 1.1 fusion.114
  182.5 1.4 convolution_add_fusion.3
  183.9 1.1 constant_dynamic-slice_fusion.6
  187.1 1.1 fusion.114
  190.8 1.4 convolution_add_fusion.3
  192.2 1.1 constant_dynamic-slice_fusion.6
  195.4 1.1 fusion.114
  199.1 1.4 convolution_add_fusion.3
  200.5 1.1 constant_dynamic-slice_fusion.6
  203.7 1.1 fusion.114
  207.4 1.4 convolution_add_fusion.3
  208.8 1.1 constant_dynamic-slice_fusion.6
  212.0 1.1 fusion.114
  215.7 1.4 convolution_add_fusion.3
  220.7 1.4 dynamic-update-slice
  222.1 65.9 %all-reduce.2 = (bf16[32]{0:T(256)(128)(2,1)S(1)}, bf16[32]{0:T(256)(128)(2,1)S(1)}) all-reduce(bf16[32]{0:T(256)(128)(2,1)S(1)} %dynamic-update-slice, bf16[32]{0:T(256)(128)(2,1)S(1)} %dynamic-update-slice.1), channel_id=1, replica_groups=mesh['req'=32,'tensor'=4] {'req'}, use_global_device_ids=true, to_apply=%add | all-reduce | flops 64 | bytes 256
  291.4 1.3 broadcast_add_fusion
  294.3 24.6 %all-gather.1 = bf16[32,1,256]{2,1,0:T(2,128)(2,1)S(1)} all-gather(bf16[1,1,256]{2,1,0:T(2,128)(2,1)S(1)} %fusion.62), channel_id=1, replica_groups=mesh['req'=32,'tensor'=4] {'req'}, dimensions={0}, use_global_device_ids=true | all-gather | bytes 16896 | tf_op jit(solution)/shard_map/all_gather | solution.py:12
  318.9 2.9 copy.44
  321.8 160.3 %while.30 = (s32[]{:T(128)}, f32[]{:T(128)}, f32[256,512]{1,0:T(8,128)S(1)}, s32[]{:T(128)}, bf16[32]{0:T(256)(128)(2,1)S(1)}, /*index=5*/bf16[32,256,512]{2,1,0...) while((s32[]{:T(128)}, f32[]{:T(128)}, ...), condition=%wide.region_8.9_spmd.clone, body=%wide.region_7.8_spmd.clone.sunk | while | flops 655885 | bytes 1313502 | solution.py:29
  482.2 5.6 %multiply_reduce_fusion = (f32[1024]{0:T(1024)S(1)}, f32[1024,512]{0,1:T(8,128)}) fusion(f32[1024,512]{0,1:T(8,128)} %copy.44, f32[1024]{0:T(1024)S(1)} %select_bitcast_fusion, f32[256,512]{1,0:T(8,128)S(1)} %get-tuple-element.200, f32[1024,256]{1,0:T(8,128)} %bitcast.119, bf16[1024,256]{1,0:T(8,128)(2,1)S(1)} %bitcast.122), kind=kOutput, calls=%fused_computation.59 | convolution fusion | flops 1613757440 | bytes 6299648 | tf_op jit(solution)/shard_map/dot_general | solution.py:139
  487.8 10.3 %convolution_convert_fusion = bf16[1024,2048]{1,0:T(8,128)(2,1)} fusion(bf16[512,2048]{1,0:T(8,128)(2,1)S(1)} %copy-done, f32[1024,512]{0,1:T(8,128)} %get-tuple-element.340, f32[512]{0:T(512)S(1)} %copy-done.8, f32[1024]{0:T(1024)S(1)} %rsqrt_multiply_fusion, bf16[1024,2048]{0,1:T(8,128)(2,1)} %bitcast.1, bf16[2048,512]{1,0:T(8,128)(2,1)} %param.20), kind=kOutput, calls=%fused_computation.56 | convolution fusion | flops 4301258752 | bytes 14686208 | tf_op jit(solution)/shard_map/dot_general | solution.py:145
  498.1 45.1 %reduce-scatter.2.cloned.1.call-done = bf16[1024,512]{1,0:T(8,128)(2,1)} async-done(((bf16[1024,2048]{1,0:T(8,128)(2,1)}), bf16[1024,512]{1,0:T(8,128)(2,1)}) %reduce-scatter.2.cloned.1.call-update) | async-done | bytes 1048592 | tf_op jit(solution)/shard_map/reduce_scatter | solution.py:146
  (396 shorter events, 162.9 us)
Async XLA Ops:
  6.5 481.3 %copy-start = (bf16[512,2048]{1,0:T(8,128)(2,1)S(1)}, bf16[512,2048]{1,0:T(8,128)(2,1)}, u32[]{:S(2)}) copy-start(bf16[512,2048]{1,0:T(8,128)(2,1)} %param.25) | copy-start | bytes 6291460
  10.6 5.1 copy-start.3
  10.7 54.0 %copy-start.2 = (bf16[2048,16]{0,1:T(8,128)(2,1)S(1)}, bf16[2048,16]{0,1:T(8,128)(2,1)}, u32[]{:S(2)}) copy-start(bf16[2048,16]{0,1:T(8,128)(2,1)} %param.21) | copy-start | bytes 196612
  10.7 54.0 %all-to-all-start = ((bf16[4,1024,512]{1,2,0:T(8,128)(2,1)}), bf16[4,1024,512]{1,2,0:T(8,128)(2,1)}, u32[]{:S(2)}, u32[]{:S(2)}) async-start(bf16[4,1024,512]{1,2,0:T(8,128)(2,1)} %stack.2), calls=%async_computation | async-start | bytes 8388608 | tf_op jit(solution)/shard_map/all_to_all | solution.py:61
  15.8 306.0 %all-gather.4.cloned.1.call-start = ((), (), s32[]{:S(2)}) async-start(), calls=%async_computation.3 | async-start | bytes 8650752 | tf_op jit(solution)/shard_map/all_gather | solution.py:12
  64.7 2.9 copy-start.7
  64.7 2.9 copy-start.9
  67.5 2.8 copy-start.5
  70.3 3.7 copy-start.4
  74.0 5.7 %copy-start.6 = (bf16[2048,256]{1,0:T(8,128)(2,1)S(1)}, bf16[2048,256]{1,0:T(8,128)(2,1)}, u32[]{:S(2)}) copy-start(bf16[2048,256]{1,0:T(8,128)(2,1)} %param.18) | copy-start | bytes 3145732
  84.0 135.3 %copy-start.10 = (u32[128]{0:T(128)S(1)}, u32[128]{0:T(128)}, u32[]{:S(2)}) copy-start(u32[128]{0:T(128)} %constant.99) | copy-start | bytes 1540
  217.9 325.4 %reduce-scatter.2.cloned.1.call-start = ((), (), s32[]{:S(2)}) async-start(), calls=%async_computation.2 | async-start | bytes 5242880 | tf_op jit(solution)/shard_map/reduce_scatter | solution.py:146
  293.3 1.0 copy-start.1
  482.2 5.6 %copy-start.8 = (f32[512]{0:T(512)S(1)}, f32[512]{0:T(512)}, u32[]{:S(2)}) copy-start(f32[512]{0:T(512)} %param.24) | copy-start | bytes 6148
Sparse Core Ops, SparseCore 0:
  218.0 54.8 all-gather.3
  498.3 44.9 reduce-scatter.1
